TPU v7x, 32 devices: a whole 2x2x4 slice. The times are simulated.
32 devices in a mesh: row: 8 (over z, y), col: 4 (over x, core).
Axes of the slice: x: 2, y: 2, z: 4, core: 2. Of those that a mesh axis runs over, the one named last changes fastest.
Arguments:
- density: float32 [4, 256, 2048], P('col', 'row'), may hold values from 0.5 to 2
- momentum: float32 [3, 4, 256, 2048], P(None, 'col', 'row'), may hold values from -6 to 6
- energy: float32 [4, 256, 2048], P('col', 'row'), may hold values from 2 to 5
Outputs:
- tendency: float32 [5, 4, 256, 2048], P(None, 'col', 'row')
All inputs are finite; a program needn't handle non-finite values.
Results may differ from a plain program's by a relative error of at most 0.000053.
Values sent between devices are 32-bit elements; how exact they have to be, the bound alone decides.
No kernel may reach another device: no remote copies, remote signals or barrier semaphores. Data moves between devices by JAX's collectives and lax.ppermute only.
A program may use at most 64 MiB of HBM per device.

v0:
```python
import jax
import jax.numpy as jnp
import numpy as np
from jax import lax
from jax.sharding import PartitionSpec as P


def operator_column(count):
    steps = np.arange(count)
    wave = 2.0 * np.pi * steps / count
    upper = (
        17.0 / 12.0 * np.sin(wave)
        + 101.0 / 300.0 * np.sin(2.0 * wave)
        + 1.0 / 300.0 * np.sin(3.0 * wave)
    )
    lower = 1.0 + np.cos(wave) + 0.1 * np.cos(2.0 * wave)
    ratio = upper / lower
    phase = 2.0 * np.pi * (steps[:, None] * steps[None, :] % count) / count
    return -np.sum(ratio[:, None] * np.sin(phase), axis=0) / count


def operator_table(count):
    column = operator_column(count)
    steps = np.arange(count)
    offsets = (steps[None, :] - steps[:, None]) % count
    return column[offsets].astype(np.float32)


def block_weights(count):
    table = operator_table(count)
    width = 128
    w_self = table[:width, :width]
    w_prev = table[:width, width : 2 * width]
    w_next = table[width : 2 * width, :width]
    return jnp.asarray(np.concatenate([w_prev, w_self, w_next], axis=1))


def compact_last(field):
    count = field.shape[-1]
    width = 128
    blocks = field.reshape(field.shape[:-1] + (count // width, width))
    parts = jnp.einsum(
        "...bj,jk->...bk", blocks, block_weights(count), precision=lax.Precision.HIGHEST
    )
    result = (
        jnp.roll(parts[..., :width], 1, axis=-2)
        + parts[..., width : 2 * width]
        + jnp.roll(parts[..., 2 * width :], -1, axis=-2)
    )
    return result.reshape(field.shape)


def compact_second(field):
    count = field.shape[-2]
    if count <= 256:
        weights = jnp.asarray(operator_table(count))
        return jnp.einsum("...jc,ji->...ic", field, weights, precision=lax.Precision.HIGHEST)
    width = 128
    blocks = field.reshape(field.shape[:-2] + (count // width, width, field.shape[-1]))
    parts = jnp.einsum(
        "...bjc,jk->...bkc", blocks, block_weights(count), precision=lax.Precision.HIGHEST
    )
    result = (
        jnp.roll(parts[..., :width, :], 1, axis=-3)
        + parts[..., width : 2 * width, :]
        + jnp.roll(parts[..., 2 * width :, :], -1, axis=-3)
    )
    return result.reshape(field.shape)


def fluxes(density, momentum, energy):
    speed = momentum / density[None]
    pressure = 0.4 * (energy - 0.5 * jnp.sum(momentum * momentum, axis=0) / density)
    enthalpy = energy + pressure
    vel_x, vel_y = (speed[0], speed[1])
    flux_x = jnp.stack(
        [
            momentum[0],
            momentum[0] * vel_x + pressure,
            momentum[1] * vel_x,
            momentum[2] * vel_x,
            enthalpy * vel_x,
        ]
    )
    flux_y = jnp.stack(
        [
            momentum[1],
            momentum[0] * vel_y,
            momentum[1] * vel_y + pressure,
            momentum[2] * vel_y,
            enthalpy * vel_y,
        ],
        axis=2,
    )
    return (flux_x, flux_y)


def local(density, momentum, energy):
    flux_x, flux_y = fluxes(density, momentum, energy)
    planes, owned, length = (flux_y.shape[0], flux_y.shape[1], flux_y.shape[3])
    packed = flux_y.reshape(planes, owned, 5 * length)
    derivative_x = compact_last(flux_x)
    y_lines = lax.all_to_all(packed, "row", split_axis=2, concat_axis=1, tiled=True)
    derivative_lines = compact_second(y_lines)
    derived = lax.all_to_all(derivative_lines, "row", split_axis=1, concat_axis=2, tiled=True)
    derivative_y = jnp.transpose(derived.reshape(planes, owned, 5, length), (2, 0, 1, 3))
    return -(derivative_x + derivative_y)


def solution(mesh):
    in_specs = (P("col", "row", None), P(None, "col", "row", None), P("col", "row", None))
    out_specs = P(None, "col", "row", None)
    return jax.shard_map(local, mesh=mesh, in_specs=in_specs, out_specs=out_specs, check_vma=False)
```

profile of v0, /device:TPU:0, one launch (start us, length us, event | category | flops | bytes accessed | tf_op | source)
XLA Modules:
  0.0 174.0 jit_solution(4821467168655819884)
XLA Ops:
  0.0 1.0 bitcast_dynamic-update-slice_fusion.9
  1.1 1.4 multiply_reduce_fusion
  2.7 3.8 %copy.31 = f32[1,32,5,2048]{1,3,2,0:T(8,128)} copy(f32[1,32,5,2048]{3,1,2,0:T(8,128)S(1)} %bitcast_dynamic-update-slice_fusion.5) | data formatting | bytes 2621440 | tf_op jit(solution)/shard_map/reshape | solution.py:101
  6.5 0.5 broadcast.11
  7.0 47.4 %reduce.1 = f32[10240,32]{1,0:T(8,128)} reduce(f32[10240,1,32]{2,1,0:T(1,128)} %bitcast.106, f32[]{:T(128)} %broadcast.11), dimensions={1}, to_apply=%bitcast.93.reduce_sub_computation | reduce | bytes 2621444
  54.4 5.3 %reshape.146 = f32[8,1,40960]{2,1,0:T(1,128)} reshape(f32[10240,32]{1,0:T(8,128)} %reduce.1) | data formatting | bytes 2621440
  59.8 38.7 %all_to_all.30 = f32[8,1,40960]{2,1,0:T(1,128)S(1)} all-to-all(f32[8,1,40960]{2,1,0:T(1,128)} %reshape.146), channel_id=1, replica_groups=mesh['row'=8,'col'=4] {'row'}, dimensions={0} | all-to-all | bytes 2621440 | tf_op jit(solution)/shard_map/all_to_all | solution.py:103
  98.4 5.2 %reduce.2 = f32[8,40960]{1,0:T(8,128)} reduce(f32[8,1,40960]{2,1,0:T(1,128)S(1)} %all_to_all.30, f32[]{:T(128)} %broadcast.11), dimensions={1}, to_apply=%all_to_all.22.reduce_sub_computation | reduce | bytes 2621444 | tf_op jit(solution)/shard_map/all_to_all | solution.py:103
  103.7 12.0 %reshape.147 = f32[10240,1,32]{2,1,0:T(1,128)} reshape(f32[8,40960]{1,0:T(8,128)} %reduce.2) | data formatting | bytes 2621440
  115.6 10.6 %copy.26 = f32[1,32,10240]{2,1,0:T(8,128)} copy(f32[1,32,10240]{1,0,2:T(1,128)} %bitcast.107) | data formatting | bytes 2621440 | tf_op jit(solution)/shard_map/all_to_all | solution.py:103
  126.2 1.5 reshape.141
  127.8 2.2 %convolution_bitcast_fusion = f32[1,256,1280]{2,1,0:T(8,128)S(1)} fusion(f32[256,256]{1,0:T(8,128)} %constant.17, f32[256,1280]{1,0:T(8,128)S(1)} %reshape.141), kind=kOutput, calls=%fused_computation | convolution fusion | flops 1006632960 | bytes 2883584 | tf_op jit(solution)/shard_map/...jc,ji->...ic/dot_general | solution.py:57
  130.0 2.4 %copy.27 = f32[1,256,1280]{2,0,1:T(1,128)} copy(f32[1,256,1280]{2,1,0:T(8,128)S(1)} %convolution_bitcast_fusion) | data formatting | bytes 2621440 | tf_op jit(solution)/shard_map/...jc,ji->...ic/transpose | solution.py:57
  132.4 4.3 %all-to-all-start.1 = ((f32[1,256,1280]{2,0,1:T(1,128)}), f32[1,256,1280]{2,0,1:T(1,128)}, u32[]{:S(2)}, u32[]{:S(2)}) async-start(f32[1,256,1280]{2,0,1:T(1,128)} %copy.27), calls=%async_computation.1 | async-start | bytes 2621440 | tf_op jit(solution)/shard_map/all_to_all | solution.py:105
  137.2 0.8 copy-done.3
  138.0 3.5 %convolution_bitcast_fusion.1 = f32[5,1,32,16,384]{4,3,2,0,1:T(8,128)S(1)} fusion(f32[5,32,16,128]{3,2,1,0:T(8,128)S(1)} %bitcast_dynamic-update-slice_fusion, f32[128,384,1,1]{1,0,3,2:T(8,128)S(1)} %copy-done.3), kind=kOutput, calls=%fused_computation.1 | convolution fusion | flops 1509949440 | bytes 5439488 | tf_op jit(solution)/shard_map/...bj,jk->...bk/dot_general | solution.py:42
  141.5 0.1 fusion.10
  141.6 0.2 fusion.9
  141.9 0.4 fusion
  142.2 0.2 reshape.137
  142.4 24.9 %all-to-all-done.1 = f32[1,256,1280]{2,0,1:T(1,128)} async-done(((f32[1,256,1280]{2,0,1:T(1,128)}), f32[1,256,1280]{2,0,1:T(1,128)}, u32[]{:S(2)}, u32[]{:S(2)}) %all-to-all-start.1) | async-done | bytes 1310752 | tf_op jit(solution)/shard_map/all_to_all | solution.py:105
  167.3 3.1 %copy.40 = f32[1,8,32,1280]{3,1,2,0:T(8,128)} copy(f32[1,8,32,1280]{3,0,2,1:T(1,128)} %bitcast.16) | data formatting | bytes 2621440 | tf_op jit(solution)/shard_map/all_to_all | solution.py:105
  170.5 1.5 reshape.140
  172.0 2.0 %fusion.1 = f32[5,1,32,2048]{3,2,1,0:T(8,128)} fusion(f32[5,1,32,2048]{3,2,1,0:T(8,128)S(1)} %reshape.137, f32[1,32,5,2048]{3,2,1,0:T(8,128)S(1)} %reshape.140), kind=kLoop, calls=%fused_computation.5 | loop fusion | flops 655360 | bytes 3932160 | tf_op jit(solution)/shard_map/neg | solution.py:107
  (23 shorter events, 0.7 us)
Async XLA Ops:
  0.0 2.5 %copy-start = (f32[3,1,32,2048]{3,2,1,0:T(8,128)S(1)}, f32[3,1,32,2048]{3,2,1,0:T(8,128)}, u32[]{:S(2)}) copy-start(f32[3,1,32,2048]{3,2,1,0:T(8,128)} %param.6) | copy-start | bytes 2359300
  1.0 1.5 copy-start.1
  1.1 1.5 copy-start.2
  132.4 35.0 %all-to-all-start.1 = ((f32[1,256,1280]{2,0,1:T(1,128)}), f32[1,256,1280]{2,0,1:T(1,128)}, u32[]{:S(2)}, u32[]{:S(2)}) async-start(f32[1,256,1280]{2,0,1:T(1,128)} %copy.27), calls=%async_computation.1 | async-start | bytes 2621440 | tf_op jit(solution)/shard_map/all_to_all | solution.py:105
  137.1 0.9 copy-start.3
where the time goes:
time: 175 us; the launch traced here: 174 us
  other arithmetic  56.7 us (32%)
  local copies, waits for them, and re-layouts  43.5 us (25%)
  blocking collectives  38.7 us (22%)
  waiting for transfers between devices  24.9 us (14%)
  matrix products  5.71 us (3%)
  starting transfers between devices  4.26 us (2%)
    unnamed x6, other arithmetic  47.7 us
    all_to_all x1, blocking collectives, local(): lax.all_to_all(packed, 'row', split_axis=2, concat_axis=1, tiled=True)  38.7 us
    all_to_all x1, waiting for transfers between devices, local(): lax.all_to_all(derivative_lines, 'row', split_axis=1, concat_axis=2, tile...  24.9 us
    unnamed x21, local copies, waits for them, and re-layouts  20 us
    all_to_all x1, local copies, waits for them, and re-layouts, local(): lax.all_to_all(packed, 'row', split_axis=2, concat_axis=1, tiled=True)  10.6 us
    all_to_all x1, other arithmetic, local(): lax.all_to_all(packed, 'row', split_axis=2, concat_axis=1, tiled=True)  5.24 us
    all_to_all x1, starting transfers between devices, local(): lax.all_to_all(derivative_lines, 'row', split_axis=1, concat_axis=2, tile...  4.26 us
    reshape x1, local copies, waits for them, and re-layouts, local(): packed = flux_y.reshape(planes, owned, 5 * length)  3.76 us
  transfers between devices with their start and end apart: 1, of which 1 were waited for; matrix products, arithmetic and copies ran while one was open for 3% of the time, Pallas kernels for 0%

commit v1 on v0

--- a/solution.py
+++ b/solution.py
@@ -3,6 +3,13 @@
 import numpy as np
 from jax import lax
 from jax.sharding import PartitionSpec as P
+
+
+def trade_parts(x, axis, split, join):
+    size = lax.axis_size(axis)
+    blocks = jnp.stack(jnp.split(x, size, axis=split), axis=0)
+    blocks = lax.all_to_all(blocks, axis, split_axis=0, concat_axis=0)
+    return jnp.concatenate(blocks, axis=join)
 
 
 def operator_column(count):
@@ -100,7 +107,7 @@
     planes, owned, length = (flux_y.shape[0], flux_y.shape[1], flux_y.shape[3])
     packed = flux_y.reshape(planes, owned, 5 * length)
     derivative_x = compact_last(flux_x)
-    y_lines = lax.all_to_all(packed, "row", split_axis=2, concat_axis=1, tiled=True)
+    y_lines = trade_parts(packed, "row", 2, 1)
     derivative_lines = compact_second(y_lines)
     derived = lax.all_to_all(derivative_lines, "row", split_axis=1, concat_axis=2, tiled=True)
     derivative_y = jnp.transpose(derived.reshape(planes, owned, 5, length), (2, 0, 1, 3))

time: 175 us -> 87.2 us (0.50)
  other arithmetic: 56.7 us -> 3.99 us
  local copies, waits for them, and re-layouts: 43.5 us -> 10 us
    unnamed x6 -> x5, other arithmetic: 47.7 us -> 0.26 us
    unnamed x21 -> x27, local copies, waits for them, and re-layouts: 20 us -> 2.27 us
    all_to_all x1 -> x0, local copies, waits for them, and re-layouts: 10.6 us -> none  [local(): lax.all_to_all(packed, 'row', split_axis=2, concat_axis=1, tiled=True)]
    all_to_all x1 -> x0, other arithmetic: 5.24 us -> none  [local(): lax.all_to_all(packed, 'row', split_axis=2, concat_axis=1, tiled=True)]
    reshape x1, local copies, waits for them, and re-layouts: 3.76 us -> 0.11 us  [local(): packed = flux_y.reshape(planes, owned, 5 * length)]
  transfers between devices with their start and end apart: 1 -> 1, of which waited for: 1 -> 1; matrix products, arithmetic and copies ran while one was open for 3% -> 6% of each run, Pallas kernels for 0% -> 0%
where the time goes in v1:
time: 87.2 us; the launch traced here: 86.9 us
  blocking collectives  38.6 us (44%)
  waiting for transfers between devices  24.9 us (29%)
  local copies, waits for them, and re-layouts  10 us (11%)
  matrix products  4.77 us (5%)
  starting transfers between devices  4.26 us (5%)
  other arithmetic  3.99 us (5%)
    all_to_all x1, blocking collectives, trade_parts(): blocks = lax.all_to_all(blocks, axis, split_axis=0, concat_axis=0)  38.6 us
    all_to_all x1, waiting for transfers between devices, local(): lax.all_to_all(derivative_lines, 'row', split_axis=1, concat_axis=2, tile...  24.9 us
    all_to_all x1, starting transfers between devices, local(): lax.all_to_all(derivative_lines, 'row', split_axis=1, concat_axis=2, tile...  4.26 us
    dot_general x1, matrix products, compact_last(): jnp.einsum('...bj,jk->...bk', blocks, block_weights(count), precision=lax...  3.51 us
    all_to_all x1, local copies, waits for them, and re-layouts, local(): lax.all_to_all(derivative_lines, 'row', split_axis=1, concat_axis=2, tile...  3.13 us
    transpose x1, local copies, waits for them, and re-layouts, compact_second(): jnp.einsum('...jc,ji->...ic', field, weights, precision=lax.Precision.HIG...  2.4 us
    unnamed x27, local copies, waits for them, and re-layouts  2.27 us
    neg x1, other arithmetic, local(): return -(derivative_x + derivative_y)  1.96 us
  transfers between devices with their start and end apart: 1, of which 1 were waited for; matrix products, arithmetic and copies ran while one was open for 6% of the time, Pallas kernels for 0%

profile of v1, /device:TPU:0, one launch (start us, length us, event | category | flops | bytes accessed | tf_op | source)
XLA Modules:
  0.0 86.9 jit_solution(5727893752712151912)
XLA Ops:
  0.0 1.0 %bitcast_dynamic-update-slice_fusion.9 = f32[1,32,5,2048]{3,1,2,0:T(8,128)S(1)} fusion(f32[3,1,32,2048]{3,2,1,0:T(8,128)} %param.6), kind=kLoop, calls=%fused_computation.21 | loop fusion | bytes 524288
  1.0 0.0 copy-start.1
  1.1 0.0 copy-start.2
  1.1 1.4 %multiply_reduce_fusion = (f32[32,2048]{1,0:T(8,128)S(1)}, f32[3,1,32,2048]{3,2,1,0:T(8,128)S(1)}) fusion(f32[3,1,32,2048]{3,2,1,0:T(8,128)} %param.6, f32[32,2048]{1,0:T(8,128)} %bitcast.154), kind=kLoop, calls=%fused_computation.7 | loop fusion | flops 524288 | bytes 2097152 | tf_op jit(solution)/shard_map/reduce_sum | solution.py:80
  2.5 0.1 bitcast_dynamic-update-slice_fusion.7
  2.7 0.1 copy.21
  3.0 0.0 copy-start.3
  3.0 38.6 %all_to_all.20 = f32[8,1,32,1280]{3,2,1,0:T(8,128)S(1)} all-to-all(f32[8,1,32,1280]{3,2,1,0:T(8,128)S(1)} %fusion.8), channel_id=1, replica_groups=mesh['row'=8,'col'=4] {'row'}, dimensions={0} | all-to-all | bytes 2621440 | tf_op jit(solution)/shard_map/all_to_all | solution.py:11
  41.6 1.3 %convolution_bitcast_fusion = f32[1,256,1280]{2,1,0:T(8,128)S(1)} fusion(f32[256,256]{1,0:T(8,128)S(1)} %copy-done.3, f32[256,1280]{1,0:T(8,128)S(1)} %bitcast.146), kind=kOutput, calls=%fused_computation | convolution fusion | flops 1006632960 | bytes 2883584 | tf_op jit(solution)/shard_map/...jc,ji->...ic/dot_general | solution.py:64
  42.9 2.4 %copy.17 = f32[1,256,1280]{2,0,1:T(1,128)} copy(f32[1,256,1280]{2,1,0:T(8,128)S(1)} %convolution_bitcast_fusion) | data formatting | bytes 2621440 | tf_op jit(solution)/shard_map/...jc,ji->...ic/transpose | solution.py:64
  45.3 4.3 %all-to-all-start.1 = ((f32[1,256,1280]{2,0,1:T(1,128)}), f32[1,256,1280]{2,0,1:T(1,128)}, u32[]{:S(2)}, u32[]{:S(2)}) async-start(f32[1,256,1280]{2,0,1:T(1,128)} %copy.17), calls=%async_computation.1 | async-start | bytes 2621440 | tf_op jit(solution)/shard_map/all_to_all | solution.py:112
  49.5 0.1 multiply_bitcast_fusion
  49.8 0.1 fusion.7
  50.0 0.0 copy-start.4
  50.1 0.8 copy-done.4
  50.9 3.5 %convolution_bitcast_fusion.1 = f32[5,1,32,16,384]{4,3,2,0,1:T(8,128)S(1)} fusion(f32[5,32,16,128]{3,2,1,0:T(8,128)S(1)} %bitcast_dynamic-update-slice_fusion, f32[128,384,1,1]{1,0,3,2:T(8,128)S(1)} %copy-done.4), kind=kOutput, calls=%fused_computation.1 | convolution fusion | flops 1509949440 | bytes 5439488 | tf_op jit(solution)/shard_map/...bj,jk->...bk/dot_general | solution.py:49
  54.4 0.1 fusion.18
  54.5 0.2 fusion.17
  54.8 0.4 fusion
  55.1 0.2 reshape.138
  55.3 24.9 %all-to-all-done.1 = f32[1,256,1280]{2,0,1:T(1,128)} async-done(((f32[1,256,1280]{2,0,1:T(1,128)}), f32[1,256,1280]{2,0,1:T(1,128)}, u32[]{:S(2)}, u32[]{:S(2)}) %all-to-all-start.1) | async-done | bytes 1310752 | tf_op jit(solution)/shard_map/all_to_all | solution.py:112
  80.3 3.1 %copy.29 = f32[1,8,32,1280]{3,1,2,0:T(8,128)} copy(f32[1,8,32,1280]{3,0,2,1:T(1,128)} %bitcast.24) | data formatting | bytes 2621440 | tf_op jit(solution)/shard_map/all_to_all | solution.py:112
  83.4 1.5 %reshape.141 = f32[1,32,5,2048]{3,2,1,0:T(8,128)S(1)} reshape(f32[1,32,8,1280]{3,2,1,0:T(8,128)} %bitcast.147) | data formatting | bytes 2621440 | tf_op jit(solution)/shard_map/reshape | solution.py:113
  84.9 2.0 %fusion.1 = f32[5,1,32,2048]{3,2,1,0:T(8,128)} fusion(f32[5,1,32,2048]{3,2,1,0:T(8,128)S(1)} %reshape.138, f32[1,32,5,2048]{3,2,1,0:T(8,128)S(1)} %reshape.141), kind=kLoop, calls=%fused_computation.5 | loop fusion | flops 655360 | bytes 3932160 | tf_op jit(solution)/shard_map/neg | solution.py:114
  (26 shorter events, 0.6 us)
Async XLA Ops:
  0.0 2.5 %copy-start = (f32[3,1,32,2048]{3,2,1,0:T(8,128)S(1)}, f32[3,1,32,2048]{3,2,1,0:T(8,128)}, u32[]{:S(2)}) copy-start(f32[3,1,32,2048]{3,2,1,0:T(8,128)} %param.6) | copy-start | bytes 2359300
  1.0 1.5 %copy-start.1 = (f32[1,32,2048]{2,1,0:T(8,128)S(1)}, f32[1,32,2048]{2,1,0:T(8,128)}, u32[]{:S(2)}) copy-start(f32[1,32,2048]{2,1,0:T(8,128)} %param.7) | copy-start | bytes 786436
  1.1 1.5 %copy-start.2 = (f32[1,32,2048]{2,1,0:T(8,128)S(1)}, f32[1,32,2048]{2,1,0:T(8,128)}, u32[]{:S(2)}) copy-start(f32[1,32,2048]{2,1,0:T(8,128)} %param.5) | copy-start | bytes 786436
  3.0 38.6 %copy-start.3 = (f32[256,256]{1,0:T(8,128)S(1)}, f32[256,256]{1,0:T(8,128)}, u32[]{:S(2)}) copy-start(f32[256,256]{1,0:T(8,128)} %constant.11.clone) | copy-start | bytes 786436
  45.3 35.0 %all-to-all-start.1 = ((f32[1,256,1280]{2,0,1:T(1,128)}), f32[1,256,1280]{2,0,1:T(1,128)}, u32[]{:S(2)}, u32[]{:S(2)}) async-start(f32[1,256,1280]{2,0,1:T(1,128)} %copy.17), calls=%async_computation.1 | async-start | bytes 2621440 | tf_op jit(solution)/shard_map/all_to_all | solution.py:112
  50.0 0.9 %copy-start.4 = (f32[128,384,1,1]{1,0,3,2:T(8,128)S(1)}, f32[128,384,1,1]{1,0,3,2:T(8,128)}, u32[]{:S(2)}) copy-start(f32[128,384,1,1]{1,0,3,2:T(8,128)} %constant.15) | copy-start | bytes 589828
